TPU v7x, 32 devices: a whole 2x2x4 slice. The times are simulated.
32 devices in a mesh: row: 4 (over y, core), col: 8 (over z, x).
Axes of the slice: x: 2, y: 2, z: 4, core: 2. Of those that a mesh axis runs over, the one named last changes fastest.
Arguments:
- node_feats: bfloat16 [8192, 256], P(('row', 'col')), may hold values from -6 to 6
- weight: bfloat16 [256, 256], replicated, may hold values from -0.375 to 0.375
- cotangent: bfloat16 [8192, 256], P(('row', 'col')), may hold values from -6 to 6
- band_tiles: bfloat16 [384, 128, 128], P(('row', 'col')), may hold values from 0 to 0.049804688
- band_coords: int32 [384, 2], P(('row', 'col')), may hold values from 0 to 5, as said below
- bound_tiles: bfloat16 [1280, 128, 128], P(('row', 'col')), may hold values from 0 to 0.049804688
- bound_coords: int32 [1280, 2], P(('row', 'col')), may hold values from 0 to 7, as said below
- bound_count: int32 [32], P(('row', 'col')), may hold values from 0 to 40, as said below
- recv_lists: int32 [32, 8], P(('row', 'col')), may hold values from -1 to 1, as said below
- send_lists: int32 [32, 8], P(('row', 'col')), may hold values from -1 to 1, as said below
- reorder: int32 [32, 256], P(('row', 'col')), may hold values from 0 to 255, each once within a row
Outputs:
- node_out: bfloat16 [8192, 256], P(('row', 'col'))
- feat_grad: bfloat16 [8192, 256], P(('row', 'col'))
- weight_grad: float32 [256, 256], replicated
Inputs may be any that keep to these rules, and one draw needn't show every extreme that they name: recv_lists[r * 8 + c, s] is a row block of device r * 8 + s, below 2, or -1 for none; it is -1 where s = c. In every row group one device receives a block from every other column. send_lists[r * 8 + s, c] equals recv_lists[r * 8 + c, s]. bound_count[d] is at least the number of entries of recv_lists[d] that are not -1; in every row group one device has all 40 slots live. `bound_coords`: pairs (row block below 2, owner column below 8); for k < bound_count[d] the owner column s of slot k has recv_lists[d, s] >= 0, and every such column is named by one of them; slots from bound_count[d] on are not used. `band_coords`: pairs (row block below 2, extended column block below (768) / 128); no pair twice on one device. `reorder`: each row is a permutation.
All inputs are finite; a program needn't handle non-finite values.
Results may differ from a plain program's by a relative error of at most 0.0095.
Values may be sent and summed in bfloat16 or wider, within the bound.
No kernel may reach another device: no remote copies, remote signals or barrier semaphores. Data moves between devices by JAX's collectives and lax.ppermute only.
A program may use at most 64 MiB of HBM per device.

v0:
```python
import jax
import jax.numpy as jnp
from jax import lax
from jax.sharding import PartitionSpec as P

BW = 256


def padded_2(cells, sides, width):
    for axis, dim in sides:
        count = lax.axis_size(axis)
        head = lax.slice_in_dim(cells, 0, width, axis=dim)
        tail = lax.slice_in_dim(cells, cells.shape[dim] - width, cells.shape[dim], axis=dim)
        cells = jnp.concatenate(
            [
                lax.ppermute(tail, axis, [(i, (i + 1) % count) for i in range(count)]),
                cells,
                lax.ppermute(head, axis, [((i + 1) % count, i) for i in range(count)]),
            ],
            axis=dim,
        )
    return cells


def split_sum(selector, terms):
    high_part = terms.astype(jnp.bfloat16)
    low_part = (terms - high_part.astype(jnp.float32)).astype(jnp.bfloat16)
    pick = selector.astype(jnp.bfloat16)
    upper_sum = jnp.einsum("rk,kaf->raf", pick, high_part, preferred_element_type=jnp.float32)
    lower_sum = jnp.einsum("rk,kaf->raf", pick, low_part, preferred_element_type=jnp.float32)
    return upper_sum + lower_sum


def on_device(
    node_feats,
    weight,
    cotangent,
    band_tiles,
    band_coords,
    bound_tiles,
    bound_coords,
    bound_count,
    recv_lists,
    send_lists,
    reorder,
):
    tile_size = band_tiles.shape[1]
    row_count = node_feats.shape[0]
    width_feat = node_feats.shape[1]
    tile_rows = row_count // tile_size
    rim_tiles = BW // tile_size
    col_tiles = tile_rows + 2 * rim_tiles
    ext_count = row_count + 2 * BW
    peers = lax.axis_size("col")
    slot_total = bound_tiles.shape[0]
    order = reorder[0]
    inverse = (
        jnp.zeros((row_count,), jnp.int32).at[order].set(jnp.arange(row_count, dtype=jnp.int32))
    )
    x_band = jnp.take(node_feats, order, axis=0)
    hidden = jnp.dot(x_band, weight, preferred_element_type=jnp.float32).astype(jnp.bfloat16)
    band_row_ids = band_coords[:, 0]
    band_col_ids = band_coords[:, 1]
    band_dense = jnp.zeros((tile_rows, tile_size, col_tiles, tile_size), jnp.bfloat16)
    band_dense = (
        band_dense.at[band_row_ids, :, band_col_ids].set(band_tiles).reshape(row_count, ext_count)
    )
    extended = padded_2(hidden, (("row", 0),), BW)
    mixed = jnp.dot(band_dense, extended, preferred_element_type=jnp.float32)
    blocks = hidden.reshape(tile_rows, tile_size, width_feat)
    giving = send_lists[0]
    outgoing = jnp.where(
        (giving >= 0)[:, None, None],
        jnp.take(blocks, jnp.maximum(giving, 0), axis=0),
        jnp.zeros((), jnp.bfloat16),
    )
    arrived = lax.all_to_all(outgoing, "col", split_axis=0, concat_axis=0, tiled=True)
    tile_range = jnp.arange(tile_rows, dtype=jnp.int32)
    live_slots = jnp.arange(slot_total, dtype=jnp.int32) < bound_count[0]
    bound_row_ids = bound_coords[:, 0]
    bound_owner = bound_coords[:, 1]
    bound_onehot = (bound_row_ids[None, :] == tile_range[:, None]) & live_slots[None, :]
    slot_rows = jnp.take(arrived, bound_owner, axis=0).reshape(slot_total * tile_size, width_feat)
    placed = jnp.einsum(
        "rk,kab->rakb",
        bound_onehot.astype(jnp.bfloat16),
        bound_tiles,
        preferred_element_type=jnp.bfloat16,
    )
    placed = placed.reshape(row_count, slot_total * tile_size)
    mixed = mixed + jnp.dot(placed, slot_rows, preferred_element_type=jnp.float32)
    out_band = jax.nn.silu(mixed).astype(jnp.bfloat16)
    node_out = jnp.take(out_band, inverse, axis=0)
    grad_band = jnp.take(cotangent, order, axis=0).astype(jnp.float32)
    sigma = jax.nn.sigmoid(mixed)
    slope = (grad_band * sigma * (1.0 + mixed * (1.0 - sigma))).astype(jnp.bfloat16)
    slope_blocks = slope.reshape(tile_rows, tile_size, width_feat)
    ext_grad = lax.dot_general(
        band_dense, slope, (((0,), (0,)), ((), ())), preferred_element_type=jnp.float32
    )
    rim_terms = jnp.concatenate([ext_grad[:BW], ext_grad[BW + row_count :]], axis=0).astype(
        jnp.bfloat16
    )
    padded = padded_2(rim_terms, (("row", 0),), BW)
    grad_hidden = ext_grad[BW : BW + row_count]
    grad_hidden = grad_hidden.at[:BW].add(padded[:BW].astype(jnp.float32))
    grad_hidden = grad_hidden.at[row_count - BW :].add(padded[3 * BW :].astype(jnp.float32))
    slot_back = jnp.einsum(
        "kab,kaf->kbf",
        bound_tiles,
        jnp.take(slope_blocks, bound_row_ids, axis=0),
        preferred_element_type=jnp.float32,
    )
    owner_range = jnp.arange(peers, dtype=jnp.int32)
    owner_onehot = (bound_owner[None, :] == owner_range[:, None]) & live_slots[None, :]
    to_owner = split_sum(owner_onehot, slot_back).astype(jnp.bfloat16)
    returned = lax.all_to_all(to_owner, "col", split_axis=0, concat_axis=0, tiled=True)
    block_onehot = (giving[None, :] == tile_range[:, None]).astype(jnp.bfloat16)
    from_peers = jnp.einsum(
        "bs,saf->baf", block_onehot, returned, preferred_element_type=jnp.float32
    )
    grad_hidden = grad_hidden + from_peers.reshape(row_count, width_feat)
    grad_round = grad_hidden.astype(jnp.bfloat16)
    partial_weight = lax.dot_general(
        x_band, grad_round, (((0,), (0,)), ((), ())), preferred_element_type=jnp.float32
    )
    nodes_all = row_count * lax.axis_size("row") * peers
    weight_grad = lax.psum(partial_weight, ("row", "col")) * nodes_all ** (-0.5)
    feat_band = lax.dot_general(
        grad_round, weight, (((1,), (1,)), ((), ())), preferred_element_type=jnp.float32
    ).astype(jnp.bfloat16)
    feat_grad = jnp.take(feat_band, inverse, axis=0)
    return (node_out, feat_grad, weight_grad)


def solution(mesh):
    in_specs = (
        P(("row", "col"), None),
        P(),
        P(("row", "col"), None),
        P(("row", "col"), None, None),
        P(("row", "col"), None),
        P(("row", "col"), None, None),
        P(("row", "col"), None),
        P(("row", "col")),
        P(("row", "col"), None),
        P(("row", "col"), None),
        P(("row", "col"), None),
    )
    out_specs = (P(("row", "col"), None), P(("row", "col"), None), P())
    return jax.shard_map(
        on_device, mesh=mesh, in_specs=in_specs, out_specs=out_specs, check_vma=False
    )
```

profile of v0, /device:TPU:0, one launch (start us, length us, event | category | flops | bytes accessed | tf_op | source)
XLA Modules:
  0.0 214.7 jit_solution(14946147041477789685)
XLA Ops:
  7.2 0.8 compare_select_fusion.2
  8.0 0.7 compare_and_fusion.1
  8.7 1.9 gather_fusion.3
  11.4 2.0 collective-permute-start.1
  15.3 0.9 select_select_fusion
  16.3 6.5 %all-to-all-start = ((bf16[8,128,256]{2,1,0:T(8,128)(2,1)}), bf16[8,128,256]{2,1,0:T(8,128)(2,1)S(1)}, u32[]{:S(2)}, u32[]{:S(2)}) async-start(bf16[8,128,256]{2,1,0:T(8,128)(2,1)} %select_select_fusion), calls=%async_computation | async-start | bytes 1048576 | tf_op jit(solution)/shard_map/all_to_all | solution.py:77
  25.2 0.8 copy.20
  26.1 1.8 gather_fusion.5
  28.0 2.0 scatter_fusion
  30.1 1.1 copy.19
  31.2 2.1 scatter_custom_fusion.1
  33.8 1.7 broadcast_multiply_fusion
  35.6 1.8 all-to-all-done
  37.3 0.7 gather_fusion.1
  38.4 1.4 copy-done.4
  39.8 0.8 fusion.1
  40.8 1.3 multiply_convert_fusion
  42.2 2.4 %gather_fusion.2 = bf16[40,128,256]{2,1,0:T(8,128)(2,1)} fusion(bf16[2,128,256]{2,1,0:T(8,128)(2,1)S(1)} %bitcast.73, s32[1024]{0:T(1024)S(1)} %pad_clamp_fusion), kind=kCustom, calls=%fused_computation.6 | custom fusion | bytes 5243040 | tf_op jit(solution)/shard_map/jit(_take)/gather | solution.py:111
  44.6 4.9 %fusion = (bf16[40,128,256]{1,2,0:T(8,128)(2,1)S(1)}, bf16[40,128,256]{1,2,0:T(8,128)(2,1)}) fusion(bf16[40,128,128]{2,1,0:T(8,128)(2,1)} %param.26, bf16[40,128,256]{2,1,0:T(8,128)(2,1)} %gather_fusion.2, pred[40]{0:T(512)(128)(4,1)S(1)} %copy-done.16), kind=kOutput, calls=%fused_computation.11 | convolution fusion | flops 342097920 | bytes 9175080 | tf_op jit(solution)/shard_map/kab,kaf->kbf/dot_general | solution.py:108
  49.5 4.7 %copy.22 = bf16[40,128,256]{2,0,1:T(8,128)(2,1)} copy(bf16[40,128,256]{1,2,0:T(8,128)(2,1)} %get-tuple-element.45) | data formatting | bytes 5242880 | tf_op jit(solution)/shard_map/convert_element_type | solution.py:26
  54.2 3.4 %copy.23 = bf16[40,128,256]{2,0,1:T(8,128)(2,1)} copy(bf16[40,128,256]{1,2,0:T(8,128)(2,1)S(1)} %get-tuple-element.44) | data formatting | bytes 5242880 | tf_op jit(solution)/shard_map/convert_element_type | solution.py:27
  57.6 2.5 %fusion.28 = f32[8,128,256]{2,0,1:T(8,128)S(1)} fusion(bf16[40,128,256]{2,0,1:T(8,128)(2,1)} %copy.22, s32[40]{0:T(128)S(1)} %get-tuple-element.50, pred[40]{0:T(512)(128)(4,1)S(1)} %copy-done.15), kind=kOutput, calls=%fused_computation.62 | convolution fusion | flops 20972160 | bytes 3670216 | tf_op jit(solution)/shard_map/rk,kaf->raf/dot_general | solution.py:29
  60.7 0.9 copy.24
  61.6 4.2 %all-to-all-start.1 = ((bf16[8,128,256]{2,1,0:T(8,128)(2,1)}), bf16[8,128,256]{2,1,0:T(8,128)(2,1)S(1)}, u32[]{:S(2)}, u32[]{:S(2)}) async-start(bf16[8,128,256]{2,1,0:T(8,128)(2,1)} %copy.24), calls=%async_computation.1 | async-start | bytes 1048576 | tf_op jit(solution)/shard_map/all_to_all | solution.py:117
  66.3 1.7 collective-permute-start.3
  68.0 1.1 gather_fusion.4
  69.2 10.8 %all-to-all-done.1 = bf16[8,128,256]{2,1,0:T(8,128)(2,1)S(1)} async-done(((bf16[8,128,256]{2,1,0:T(8,128)(2,1)}), bf16[8,128,256]{2,1,0:T(8,128)(2,1)S(1)}, u32[]{:S(2)}, u32[]{:S(2)}) %all-to-all-start.1) | async-done | bytes 524320 | tf_op jit(solution)/shard_map/all_to_all | solution.py:117
  80.7 1.0 fusion.24
  81.7 1.1 gather_fusion.6
  82.9 0.8 broadcast_select_fusion.1
  83.7 122.5 %all-reduce.2.cloned.1.call-done = f32[256,256]{1,0:T(8,128)} async-done(((f32[256,256]{1,0:T(8,128)}), f32[256,256]{1,0:T(8,128)}) %all-reduce.2.cloned.1.call-update) | async-done | bytes 262160 | tf_op jit(solution)/shard_map/psum | solution.py:128
  206.1 1.7 broadcast_multiply_fusion.1
  (78 shorter events, 7.3 us)
Async XLA Ops:
  7.2 3.4 %copy-start = (bf16[256,256]{1,0:T(8,128)(2,1)S(1)}, bf16[256,256]{1,0:T(8,128)(2,1)}, u32[]{:S(2)}) copy-start(bf16[256,256]{1,0:T(8,128)(2,1)} %param.22) | copy-start | bytes 393220
  7.2 15.6 %copy-start.11 = (s32[1,256]{1,0:T(1,128)S(1)}, s32[1,256]{1,0:T(1,128)}, u32[]{:S(2)}) copy-start(s32[1,256]{1,0:T(1,128)} %param.30) | copy-start | bytes 3076
  7.2 16.2 %copy-start.9 = (s32[40,2]{0,1:T(2,128)S(1)}, s32[40,2]{0,1:T(2,128)}, u32[]{:S(2)}) copy-start(s32[40,2]{0,1:T(2,128)} %param.27) | copy-start | bytes 964
  7.2 17.4 %copy-start.21 = (s32[12,2]{0,1:T(2,128)S(1)}, s32[12,2]{0,1:T(2,128)}, u32[]{:S(2)}) copy-start(s32[12,2]{0,1:T(2,128)} %param.25) | copy-start | bytes 292
  7.2 18.0 %copy-start.3 = (bf16[40,128,128]{2,1,0:T(8,128)(2,1)S(1)}, bf16[40,128,128]{2,1,0:T(8,128)(2,1)}, u32[]{:S(2)}) copy-start(bf16[40,128,128]{2,1,0:T(8,128)(2,1)} %param.26) | copy-start | bytes 3932164
  8.7 5.3 %copy-start.12 = (pred[256]{0:T(512)(128)(4,1)}, pred[256]{0:T(512)(128)(4,1)S(1)}, u32[]{:S(2)}) copy-start(pred[256]{0:T(512)(128)(4,1)S(1)} %compare_and_fusion.1) | copy-start | bytes 772
  10.6 4.1 %copy-start.6 = (bf16[256,256]{1,0:T(8,128)(2,1)}, bf16[256,256]{1,0:T(8,128)(2,1)S(1)}, u32[]{:S(2)}) copy-start(bf16[256,256]{1,0:T(8,128)(2,1)S(1)} %gather_fusion.3) | copy-start | bytes 393220
  10.9 29.8 %collective-permute-start = (bf16[256,256]{1,0:T(8,128)(2,1)S(1)}, bf16[256,256]{1,0:T(8,128)(2,1)}, u32[]{:S(2)}, u32[]{:S(2)}) collective-permute-start(bf16[256,256]{1,0:T(8,128)(2,1)S(1)} %convolution_convert_fusion.1), channel_id=1, source_target_pairs={{0,8},{8,16},{16,24},{24,0},{1,9},{9,17},{17,25},{25,1},{2,10},{10... | collective-permute-start | bytes 393224 | tf_op jit(solution)/shard_map/ppermute | solution.py:16
  11.4 29.3 %collective-permute-start.1 = (bf16[256,256]{1,0:T(8,128)(2,1)S(1)}, bf16[256,256]{1,0:T(8,128)(2,1)}, u32[]{:S(2)}, u32[]{:S(2)}) collective-permute-start(bf16[256,256]{1,0:T(8,128)(2,1)S(1)} %convolution_convert_fusion.1), channel_id=1, source_target_pairs={{8,0},{16,8},{24,16},{0,24},{9,1},{17,9},{25,17},{1,25},{10,2},{18... | collective-permute-start | bytes 393224 | tf_op jit(solution)/shard_map/ppermute | solution.py:18
  15.3 10.8 %copy-start.2 = (bf16[256,256]{1,0:T(8,128)(2,1)S(1)}, bf16[256,256]{1,0:T(8,128)(2,1)}, u32[]{:S(2)}) copy-start(bf16[256,256]{1,0:T(8,128)(2,1)} %param.23) | copy-start | bytes 393220
  16.3 21.1 %all-to-all-start = ((bf16[8,128,256]{2,1,0:T(8,128)(2,1)}), bf16[8,128,256]{2,1,0:T(8,128)(2,1)S(1)}, u32[]{:S(2)}, u32[]{:S(2)}) async-start(bf16[8,128,256]{2,1,0:T(8,128)(2,1)} %select_select_fusion), calls=%async_computation | async-start | bytes 1048576 | tf_op jit(solution)/shard_map/all_to_all | solution.py:77
  26.1 7.2 %copy-start.17 = (s32[40]{0:T(128)S(1)}, s32[40]{0:T(128)}, u32[]{:S(2)}) copy-start(s32[40]{0:T(128)} %get-tuple-element.51) | copy-start | bytes 484
  26.1 7.2 %copy-start.14 = (pred[40]{0:T(512)(128)(4,1)S(1)}, pred[40]{0:T(512)(128)(4,1)}, u32[]{:S(2)}) copy-start(pred[40]{0:T(512)(128)(4,1)} %iota_compare_fusion.1) | copy-start | bytes 124
  26.1 7.2 %copy-start.19 = (s32[40]{0:T(128)S(1)}, s32[40]{0:T(128)}, u32[]{:S(2)}) copy-start(s32[40]{0:T(128)} %get-tuple-element.53) | copy-start | bytes 484
  26.1 7.2 %copy-start.10 = (s32[40,2]{0,1:T(2,128)S(1)}, s32[40,2]{0,1:T(2,128)}, u32[]{:S(2)}) copy-start(s32[40,2]{0,1:T(2,128)} %param.27) | copy-start | bytes 964
  38.1 1.7 copy-start.4
  39.8 1.0 copy-start.5
  39.8 1.0 copy-start.8
  39.8 1.0 copy-start.13
  42.2 2.4 %copy-start.16 = (pred[40]{0:T(512)(128)(4,1)S(1)}, pred[40]{0:T(512)(128)(4,1)}, u32[]{:S(2)}) copy-start(pred[40]{0:T(512)(128)(4,1)} %get-tuple-element.54) | copy-start | bytes 124
  54.2 3.4 %copy-start.15 = (pred[40]{0:T(512)(128)(4,1)S(1)}, pred[40]{0:T(512)(128)(4,1)}, u32[]{:S(2)}) copy-start(pred[40]{0:T(512)(128)(4,1)} %iota_compare_fusion.1) | copy-start | bytes 124
  57.6 2.5 %copy-start.1 = (bf16[40,128,256]{2,0,1:T(8,128)(2,1)S(1)}, bf16[40,128,256]{2,0,1:T(8,128)(2,1)}, u32[]{:S(2)}) copy-start(bf16[40,128,256]{2,0,1:T(8,128)(2,1)} %copy.23) | copy-start | bytes 7864324
  60.1 5.8 %copy-start.18 = (s32[256]{0:T(256)S(1)}, s32[256]{0:T(256)}, u32[]{:S(2)}) copy-start(s32[256]{0:T(256)} %scatter_custom_fusion.1) | copy-start | bytes 3076
  60.7 19.3 %copy-start.20 = (s32[1,8]{1,0:T(1,128)S(1)}, s32[1,8]{1,0:T(1,128)}, u32[]{:S(2)}) copy-start(s32[1,8]{1,0:T(1,128)} %param.29) | copy-start | bytes 100
  61.6 18.4 %all-to-all-start.1 = ((bf16[8,128,256]{2,1,0:T(8,128)(2,1)}), bf16[8,128,256]{2,1,0:T(8,128)(2,1)S(1)}, u32[]{:S(2)}, u32[]{:S(2)}) async-start(bf16[8,128,256]{2,1,0:T(8,128)(2,1)} %copy.24), calls=%async_computation.1 | async-start | bytes 1048576 | tf_op jit(solution)/shard_map/all_to_all | solution.py:117
  65.8 140.3 %all-reduce.2.cloned.1.call-start = ((), (), s32[]{:S(2)}) async-start(), calls=%async_computation.2 | async-start | bytes 524288 | tf_op jit(solution)/shard_map/psum | solution.py:128
  65.9 14.8 %copy-start.7 = (bf16[256,256]{1,0:T(8,128)(2,1)S(1)}, bf16[256,256]{1,0:T(8,128)(2,1)}, u32[]{:S(2)}) copy-start(bf16[256,256]{1,0:T(8,128)(2,1)} %copy-done.6) | copy-start | bytes 393220
  66.2 14.1 %collective-permute-start.2 = (bf16[256,256]{1,0:T(8,128)(2,1)S(1)}, bf16[256,256]{1,0:T(8,128)(2,1)S(1)}, u32[]{:S(2)}, u32[]{:S(2)}) collective-permute-start(bf16[256,256]{1,0:T(8,128)(2,1)S(1)} %get-tuple-element.46), channel_id=1, source_target_pairs={{0,8},{8,16},{16,24},{24,0},{1,9},{9,17},{17,25},{25,1},{2,10},{10... | collective-permute-start | bytes 393224 | tf_op jit(solution)/shard_map/ppermute | solution.py:16
  66.3 14.1 %collective-permute-start.3 = (bf16[256,256]{1,0:T(8,128)(2,1)S(1)}, bf16[256,256]{1,0:T(8,128)(2,1)S(1)}, u32[]{:S(2)}, u32[]{:S(2)}) collective-permute-start(bf16[256,256]{1,0:T(8,128)(2,1)S(1)} %get-tuple-element.47), channel_id=1, source_target_pairs={{8,0},{16,8},{24,16},{0,24},{9,1},{17,9},{25,17},{1,25},{10,2},{18... | collective-permute-start | bytes 393224 | tf_op jit(solution)/shard_map/ppermute | solution.py:18
Sparse Core Ops, SparseCore 0:
  83.0 123.1 all-reduce.1
where the time goes:
time: 215 us
  waiting for transfers between devices  135 us (63%)
  local copies, waits for them, and re-layouts  26.5 us (12%)
  starting transfers between devices  15.1 us (7%)
  between operations  15.1 us (7%)
  matrix products  12.3 us (6%)
  other arithmetic  10.6 us (5%)
    psum x1, waiting for transfers between devices, on_device(): weight_grad = lax.psum(partial_weight, ('row', 'col')) * nodes_all ** (-0.5)  122 us
    all_to_all x1, waiting for transfers between devices, on_device(): lax.all_to_all(to_owner, 'col', split_axis=0, concat_axis=0, tiled=True)  10.8 us
    all_to_all x1, starting transfers between devices, on_device(): lax.all_to_all(outgoing, 'col', split_axis=0, concat_axis=0, tiled=True)  6.53 us
    dot_general x1, matrix products, on_device(): jnp.einsum('kab,kaf->kbf', bound_tiles, jnp.take(slope_blocks, bound_row_...  4.94 us
    convert_element_type x1, local copies, waits for them, and re-layouts, split_sum(): high_part = terms.astype(jnp.bfloat16)  4.69 us
  transfers between devices with their start and end apart: 7, of which 3 were waited for; matrix products, arithmetic and copies ran while one was open for 9% of the time, Pallas kernels for 0%

commit v1 on v0

--- a/solution.py
+++ b/solution.py
@@ -2,6 +2,7 @@
 import jax.numpy as jnp
 from jax import lax
 from jax.sharding import PartitionSpec as P
+from jax.lax import psum
 
 BW = 256
 
@@ -125,7 +126,7 @@
         x_band, grad_round, (((0,), (0,)), ((), ())), preferred_element_type=jnp.float32
     )
     nodes_all = row_count * lax.axis_size("row") * peers
-    weight_grad = lax.psum(partial_weight, ("row", "col")) * nodes_all ** (-0.5)
+    weight_grad = psum(psum(partial_weight, axis_name="col"), axis_name="row") * nodes_all ** (-0.5)
     feat_band = lax.dot_general(
         grad_round, weight, (((1,), (1,)), ((), ())), preferred_element_type=jnp.float32
     ).astype(jnp.bfloat16)

time: 215 us -> 193 us (0.90)
  waiting for transfers between devices: 135 us -> 113 us
    psum x1 -> x2, waiting for transfers between devices: 122 us -> 99.1 us  [the longest x1 66.3 us: on_device(): psum(partial_weight, axis_name='col')]
  transfers between devices with their start and end apart: 7 -> 8, of which waited for: 3 -> 4; matrix products, arithmetic and copies ran while one was open for 9% -> 11% of each run, Pallas kernels for 0% -> 0%
where the time goes in v1:
time: 193 us
  waiting for transfers between devices  113 us (59%)
  local copies, waits for them, and re-layouts  26.5 us (14%)
  starting transfers between devices  15.3 us (8%)
  between operations  15.1 us (8%)
  matrix products  12.3 us (6%)
  other arithmetic  10.6 us (5%)
    psum x1, waiting for transfers between devices, on_device(): psum(partial_weight, axis_name='col')  66.3 us
    psum x1, waiting for transfers between devices, on_device(): psum(psum(partial_weight, axis_name='col'), axis_name='row')  32.9 us
    all_to_all x1, waiting for transfers between devices, on_device(): lax.all_to_all(to_owner, 'col', split_axis=0, concat_axis=0, tiled=True)  11.9 us
    all_to_all x1, starting transfers between devices, on_device(): lax.all_to_all(outgoing, 'col', split_axis=0, concat_axis=0, tiled=True)  6.53 us
    dot_general x1, matrix products, on_device(): jnp.einsum('kab,kaf->kbf', bound_tiles, jnp.take(slope_blocks, bound_row_...  4.94 us
    convert_element_type x1, local copies, waits for them, and re-layouts, split_sum(): high_part = terms.astype(jnp.bfloat16)  4.69 us
    all_to_all x1, starting transfers between devices, on_device(): lax.all_to_all(to_owner, 'col', split_axis=0, concat_axis=0, tiled=True)  4.37 us
  transfers between devices with their start and end apart: 8, of which 4 were waited for; matrix products, arithmetic and copies ran while one was open for 11% of the time, Pallas kernels for 0%

profile of v1, /device:TPU:0, one launch (start us, length us, event | category | flops | bytes accessed | tf_op | source)
XLA Modules:
  0.0 192.7 jit_solution(15419963762835371703)
XLA Ops:
  7.2 0.8 compare_select_fusion.2
  8.7 1.9 gather_fusion.3
  11.4 2.0 %collective-permute-start.1 = (bf16[256,256]{1,0:T(8,128)(2,1)S(1)}, bf16[256,256]{1,0:T(8,128)(2,1)}, u32[]{:S(2)}, u32[]{:S(2)}) collective-permute-start(bf16[256,256]{1,0:T(8,128)(2,1)S(1)} %convolution_convert_fusion.1), channel_id=1, source_target_pairs={{8,0},{16,8},{24,16},{0,24},{9,1},{17,9},{25,17},{1,25},{10,2},{18... | collective-permute-start | bytes 393224 | tf_op jit(solution)/shard_map/ppermute | solution.py:19
  15.3 0.9 select_select_fusion
  16.3 6.5 %all-to-all-start = ((bf16[8,128,256]{2,1,0:T(8,128)(2,1)}), bf16[8,128,256]{2,1,0:T(8,128)(2,1)S(1)}, u32[]{:S(2)}, u32[]{:S(2)}) async-start(bf16[8,128,256]{2,1,0:T(8,128)(2,1)} %select_select_fusion), calls=%async_computation | async-start | bytes 1048576 | tf_op jit(solution)/shard_map/all_to_all | solution.py:78
  25.2 0.8 copy.20
  26.1 1.8 gather_fusion.5
  28.0 2.0 %scatter_fusion = bf16[2,128,6,128]{3,1,2,0:T(8,128)(2,1)S(1)} fusion(bf16[2,128,6,128]{3,1,2,0:T(8,128)(2,1)S(1)} %broadcast_in_dim.61, s32[12]{0:T(128)S(1)} %fusion.42, bf16[12,128,128]{2,1,0:T(8,128)(2,1)} %param.24), kind=kCustom, calls=%fused_computation.7 | custom fusion | bytes 1179744 | tf_op jit(solution)/shard_map/scatter | solution.py:67
  30.1 1.1 copy.19
  31.2 2.1 %scatter_custom_fusion.1 = s32[256]{0:T(256)} fusion(s32[256]{0:T(256)} %bitcast.81, s32[256]{0:T(256)S(1)} %iota.18, s32[]{:T(128)} %constant.131.clone.1), kind=kCustom, calls=%fused_computation.85 | custom fusion | bytes 1536 | tf_op jit(solution)/shard_map/scatter | solution.py:59
  33.8 1.7 broadcast_multiply_fusion
  35.6 1.8 all-to-all-done
  37.3 0.7 gather_fusion.1
  38.4 1.4 copy-done.4
  39.8 0.8 fusion.1
  40.8 1.3 multiply_convert_fusion
  42.2 2.4 %gather_fusion.2 = bf16[40,128,256]{2,1,0:T(8,128)(2,1)} fusion(bf16[2,128,256]{2,1,0:T(8,128)(2,1)S(1)} %bitcast.73, s32[1024]{0:T(1024)S(1)} %pad_clamp_fusion), kind=kCustom, calls=%fused_computation.6 | custom fusion | bytes 5243040 | tf_op jit(solution)/shard_map/jit(_take)/gather | solution.py:112
  44.6 4.9 %fusion = (bf16[40,128,256]{1,2,0:T(8,128)(2,1)S(1)}, bf16[40,128,256]{1,2,0:T(8,128)(2,1)}) fusion(bf16[40,128,128]{2,1,0:T(8,128)(2,1)} %param.26, bf16[40,128,256]{2,1,0:T(8,128)(2,1)} %gather_fusion.2, pred[40]{0:T(512)(128)(4,1)S(1)} %copy-done.16), kind=kOutput, calls=%fused_computation.11 | convolution fusion | flops 342097920 | bytes 9175080 | tf_op jit(solution)/shard_map/kab,kaf->kbf/dot_general | solution.py:109
  49.5 4.7 %copy.22 = bf16[40,128,256]{2,0,1:T(8,128)(2,1)} copy(bf16[40,128,256]{1,2,0:T(8,128)(2,1)} %get-tuple-element.45) | data formatting | bytes 5242880 | tf_op jit(solution)/shard_map/convert_element_type | solution.py:27
  54.2 3.4 %copy.23 = bf16[40,128,256]{2,0,1:T(8,128)(2,1)} copy(bf16[40,128,256]{1,2,0:T(8,128)(2,1)S(1)} %get-tuple-element.44) | data formatting | bytes 5242880 | tf_op jit(solution)/shard_map/convert_element_type | solution.py:28
  57.6 2.5 %fusion.28 = f32[8,128,256]{2,0,1:T(8,128)S(1)} fusion(bf16[40,128,256]{2,0,1:T(8,128)(2,1)} %copy.22, s32[40]{0:T(128)S(1)} %get-tuple-element.50, pred[40]{0:T(512)(128)(4,1)S(1)} %copy-done.15), kind=kOutput, calls=%fused_computation.62 | convolution fusion | flops 20972160 | bytes 3670216 | tf_op jit(solution)/shard_map/rk,kaf->raf/dot_general | solution.py:30
  60.7 0.9 copy.24
  61.6 4.4 %all-to-all-start.1 = ((bf16[8,128,256]{2,1,0:T(8,128)(2,1)}), bf16[8,128,256]{2,1,0:T(8,128)(2,1)S(1)}, u32[]{:S(2)}, u32[]{:S(2)}) async-start(bf16[8,128,256]{2,1,0:T(8,128)(2,1)} %copy.24), calls=%async_computation.1 | async-start | bytes 1048576 | tf_op jit(solution)/shard_map/all_to_all | solution.py:118
  66.4 1.7 collective-permute-start.3
  68.1 11.9 %all-to-all-done.1 = bf16[8,128,256]{2,1,0:T(8,128)(2,1)S(1)} async-done(((bf16[8,128,256]{2,1,0:T(8,128)(2,1)}), bf16[8,128,256]{2,1,0:T(8,128)(2,1)S(1)}, u32[]{:S(2)}, u32[]{:S(2)}) %all-to-all-start.1) | async-done | bytes 524320 | tf_op jit(solution)/shard_map/all_to_all | solution.py:118
  80.6 1.0 fusion.24
  81.7 1.2 gather_fusion.4
  83.1 1.2 gather_fusion.6
  84.2 66.3 %all-reduce.3.cloned.1.call-done = f32[256,256]{1,0:T(8,128)} async-done(((f32[256,256]{1,0:T(8,128)}), f32[256,256]{1,0:T(8,128)}) %all-reduce.3.cloned.1.call-update) | async-done | bytes 262160 | tf_op jit(solution)/shard_map/psum | solution.py:129
  150.5 0.8 broadcast_select_fusion.1
  151.3 32.9 %all-reduce.5.cloned.1.call-done = f32[256,256]{1,0:T(8,128)} async-done(((f32[256,256]{1,0:T(8,128)}), f32[256,256]{1,0:T(8,128)}) %all-reduce.5.cloned.1.call-update) | async-done | bytes 262160 | tf_op jit(solution)/shard_map/psum | solution.py:129
  184.2 1.7 broadcast_multiply_fusion.1
  (81 shorter events, 8.0 us)
Async XLA Ops:
  7.2 3.4 %copy-start = (bf16[256,256]{1,0:T(8,128)(2,1)S(1)}, bf16[256,256]{1,0:T(8,128)(2,1)}, u32[]{:S(2)}) copy-start(bf16[256,256]{1,0:T(8,128)(2,1)} %param.22) | copy-start | bytes 393220
  7.2 15.6 %copy-start.11 = (s32[1,256]{1,0:T(1,128)S(1)}, s32[1,256]{1,0:T(1,128)}, u32[]{:S(2)}) copy-start(s32[1,256]{1,0:T(1,128)} %param.30) | copy-start | bytes 3076
  7.2 16.2 %copy-start.9 = (s32[40,2]{0,1:T(2,128)S(1)}, s32[40,2]{0,1:T(2,128)}, u32[]{:S(2)}) copy-start(s32[40,2]{0,1:T(2,128)} %param.27) | copy-start | bytes 964
  7.2 17.4 %copy-start.21 = (s32[12,2]{0,1:T(2,128)S(1)}, s32[12,2]{0,1:T(2,128)}, u32[]{:S(2)}) copy-start(s32[12,2]{0,1:T(2,128)} %param.25) | copy-start | bytes 292
  7.2 18.0 %copy-start.3 = (bf16[40,128,128]{2,1,0:T(8,128)(2,1)S(1)}, bf16[40,128,128]{2,1,0:T(8,128)(2,1)}, u32[]{:S(2)}) copy-start(bf16[40,128,128]{2,1,0:T(8,128)(2,1)} %param.26) | copy-start | bytes 3932164
  8.7 5.3 %copy-start.12 = (pred[256]{0:T(512)(128)(4,1)}, pred[256]{0:T(512)(128)(4,1)S(1)}, u32[]{:S(2)}) copy-start(pred[256]{0:T(512)(128)(4,1)S(1)} %compare_and_fusion.1) | copy-start | bytes 772
  10.6 4.1 %copy-start.6 = (bf16[256,256]{1,0:T(8,128)(2,1)}, bf16[256,256]{1,0:T(8,128)(2,1)S(1)}, u32[]{:S(2)}) copy-start(bf16[256,256]{1,0:T(8,128)(2,1)S(1)} %gather_fusion.3) | copy-start | bytes 393220
  10.9 29.8 %collective-permute-start = (bf16[256,256]{1,0:T(8,128)(2,1)S(1)}, bf16[256,256]{1,0:T(8,128)(2,1)}, u32[]{:S(2)}, u32[]{:S(2)}) collective-permute-start(bf16[256,256]{1,0:T(8,128)(2,1)S(1)} %convolution_convert_fusion.1), channel_id=1, source_target_pairs={{0,8},{8,16},{16,24},{24,0},{1,9},{9,17},{17,25},{25,1},{2,10},{10... | collective-permute-start | bytes 393224 | tf_op jit(solution)/shard_map/ppermute | solution.py:17
  11.4 29.3 %collective-permute-start.1 = (bf16[256,256]{1,0:T(8,128)(2,1)S(1)}, bf16[256,256]{1,0:T(8,128)(2,1)}, u32[]{:S(2)}, u32[]{:S(2)}) collective-permute-start(bf16[256,256]{1,0:T(8,128)(2,1)S(1)} %convolution_convert_fusion.1), channel_id=1, source_target_pairs={{8,0},{16,8},{24,16},{0,24},{9,1},{17,9},{25,17},{1,25},{10,2},{18... | collective-permute-start | bytes 393224 | tf_op jit(solution)/shard_map/ppermute | solution.py:19
  15.3 10.8 %copy-start.2 = (bf16[256,256]{1,0:T(8,128)(2,1)S(1)}, bf16[256,256]{1,0:T(8,128)(2,1)}, u32[]{:S(2)}) copy-start(bf16[256,256]{1,0:T(8,128)(2,1)} %param.23) | copy-start | bytes 393220
  16.3 21.1 %all-to-all-start = ((bf16[8,128,256]{2,1,0:T(8,128)(2,1)}), bf16[8,128,256]{2,1,0:T(8,128)(2,1)S(1)}, u32[]{:S(2)}, u32[]{:S(2)}) async-start(bf16[8,128,256]{2,1,0:T(8,128)(2,1)} %select_select_fusion), calls=%async_computation | async-start | bytes 1048576 | tf_op jit(solution)/shard_map/all_to_all | solution.py:78
  26.1 7.2 %copy-start.17 = (s32[40]{0:T(128)S(1)}, s32[40]{0:T(128)}, u32[]{:S(2)}) copy-start(s32[40]{0:T(128)} %get-tuple-element.51) | copy-start | bytes 484
  26.1 7.2 %copy-start.14 = (pred[40]{0:T(512)(128)(4,1)S(1)}, pred[40]{0:T(512)(128)(4,1)}, u32[]{:S(2)}) copy-start(pred[40]{0:T(512)(128)(4,1)} %iota_compare_fusion.1) | copy-start | bytes 124
  26.1 7.2 %copy-start.19 = (s32[40]{0:T(128)S(1)}, s32[40]{0:T(128)}, u32[]{:S(2)}) copy-start(s32[40]{0:T(128)} %get-tuple-element.53) | copy-start | bytes 484
  26.1 7.2 %copy-start.10 = (s32[40,2]{0,1:T(2,128)S(1)}, s32[40,2]{0,1:T(2,128)}, u32[]{:S(2)}) copy-start(s32[40,2]{0,1:T(2,128)} %param.27) | copy-start | bytes 964
  38.1 1.7 copy-start.4
  39.8 1.0 copy-start.5
  39.8 1.0 copy-start.8
  39.8 1.0 copy-start.13
  42.2 2.4 %copy-start.16 = (pred[40]{0:T(512)(128)(4,1)S(1)}, pred[40]{0:T(512)(128)(4,1)}, u32[]{:S(2)}) copy-start(pred[40]{0:T(512)(128)(4,1)} %get-tuple-element.54) | copy-start | bytes 124
  54.2 3.4 %copy-start.15 = (pred[40]{0:T(512)(128)(4,1)S(1)}, pred[40]{0:T(512)(128)(4,1)}, u32[]{:S(2)}) copy-start(pred[40]{0:T(512)(128)(4,1)} %iota_compare_fusion.1) | copy-start | bytes 124
  57.6 2.5 %copy-start.1 = (bf16[40,128,256]{2,0,1:T(8,128)(2,1)S(1)}, bf16[40,128,256]{2,0,1:T(8,128)(2,1)}, u32[]{:S(2)}) copy-start(bf16[40,128,256]{2,0,1:T(8,128)(2,1)} %copy.23) | copy-start | bytes 7864324
  60.1 5.9 %copy-start.18 = (s32[256]{0:T(256)S(1)}, s32[256]{0:T(256)}, u32[]{:S(2)}) copy-start(s32[256]{0:T(256)} %scatter_custom_fusion.1) | copy-start | bytes 3076
  60.7 19.4 %copy-start.20 = (s32[1,8]{1,0:T(1,128)S(1)}, s32[1,8]{1,0:T(1,128)}, u32[]{:S(2)}) copy-start(s32[1,8]{1,0:T(1,128)} %param.29) | copy-start | bytes 100
  61.6 19.0 %copy-start.7 = (bf16[256,256]{1,0:T(8,128)(2,1)S(1)}, bf16[256,256]{1,0:T(8,128)(2,1)}, u32[]{:S(2)}) copy-start(bf16[256,256]{1,0:T(8,128)(2,1)} %copy-done.6) | copy-start | bytes 393220
  61.6 18.5 %all-to-all-start.1 = ((bf16[8,128,256]{2,1,0:T(8,128)(2,1)}), bf16[8,128,256]{2,1,0:T(8,128)(2,1)S(1)}, u32[]{:S(2)}, u32[]{:S(2)}) async-start(bf16[8,128,256]{2,1,0:T(8,128)(2,1)} %copy.24), calls=%async_computation.1 | async-start | bytes 1048576 | tf_op jit(solution)/shard_map/all_to_all | solution.py:118
  65.9 84.5 %all-reduce.3.cloned.1.call-start = ((), (), s32[]{:S(2)}) async-start(), calls=%async_computation.2 | async-start | bytes 524288 | tf_op jit(solution)/shard_map/psum | solution.py:129
  66.3 14.2 %collective-permute-start.2 = (bf16[256,256]{1,0:T(8,128)(2,1)S(1)}, bf16[256,256]{1,0:T(8,128)(2,1)S(1)}, u32[]{:S(2)}, u32[]{:S(2)}) collective-permute-start(bf16[256,256]{1,0:T(8,128)(2,1)S(1)} %get-tuple-element.46), channel_id=1, source_target_pairs={{0,8},{8,16},{16,24},{24,0},{1,9},{9,17},{17,25},{25,1},{2,10},{10... | collective-permute-start | bytes 393224 | tf_op jit(solution)/shard_map/ppermute | solution.py:17
  66.4 14.1 %collective-permute-start.3 = (bf16[256,256]{1,0:T(8,128)(2,1)S(1)}, bf16[256,256]{1,0:T(8,128)(2,1)S(1)}, u32[]{:S(2)}, u32[]{:S(2)}) collective-permute-start(bf16[256,256]{1,0:T(8,128)(2,1)S(1)} %get-tuple-element.47), channel_id=1, source_target_pairs={{8,0},{16,8},{24,16},{0,24},{9,1},{17,9},{25,17},{1,25},{10,2},{18... | collective-permute-start | bytes 393224 | tf_op jit(solution)/shard_map/ppermute | solution.py:19
  81.6 102.6 %all-reduce.5.cloned.1.call-start = ((), (), s32[]{:S(2)}) async-start(), calls=%async_computation.3 | async-start | bytes 524288 | tf_op jit(solution)/shard_map/psum | solution.py:129
Sparse Core Ops, SparseCore 0:
  81.7 68.6 all-reduce.2
  152.9 31.2 all-reduce.4
